TPU v7x, 32 devices: a whole 2x2x4 slice. The times are simulated.
32 devices in a mesh: dp: 8 (over y, x, core), blk: 4 (over z).
Axes of the slice: x: 2, y: 2, z: 4, core: 2. Of those that a mesh axis runs over, the one named last changes fastest.
Arguments:
- spans: bfloat16 [40960, 1024], P(('dp', 'blk')), may hold values from -6 to 6
- span_counts: int32 [32], P(('dp', 'blk')), may hold values from 16 to 1232, as said below
- session_ids: int32 [40960], P(('dp', 'blk')), may hold values from 0 to 15, as said below
- destinations: int32 [40960], P(('dp', 'blk')), may hold values from 0 to 7, as said below
- expert_weight: bfloat16 [8, 1024, 4096], P('dp'), may hold values from -0.1875 to 0.1875
- norm_gain: float32 [1024], replicated, may hold values from 0.1 to 1.9
- queries: bfloat16 [28672, 4096], P(('dp', 'blk')), may hold values from -6 to 6
- positives: int32 [28672], P(('dp', 'blk')), may hold values from 0 to 63
Outputs:
- loss_rows: float32 [28672], P(('dp', 'blk'))
- grad_queries: bfloat16 [28672, 4096], P(('dp', 'blk'))
- grad_sessions: float32 [512, 4096], P(('dp', 'blk'))
Inputs may be any that keep to these rules, and one draw needn't show every extreme that they name: `span_counts`: for each blk index the counts of the devices along dp sum to 2560, and one of them has the largest value. `destinations`: the live rows of the devices that share a blk index, in order of dp index and then of row, name the experts in cyclic order from a drawn start: each expert receives exactly 320 live rows of its blk index, and a device sends at most 154 live rows to one expert, the device with the largest count exactly 154 to each. Rows at or after a device's count name any expert. `session_ids`: on each device the ids of the live rows never fall, begin at 0 and take every value; rows at or after the count carry any id.
All inputs are finite; a program needn't handle non-finite values.
Results may differ from a plain program's by a relative error of at most 0.0072.
Values may be sent and summed in bfloat16 or wider, within the bound.
No kernel may reach another device: no remote copies, remote signals or barrier semaphores. Data moves between devices by JAX's collectives and lax.ppermute only.
A program may use at most 128 MiB of HBM per device.

v0:
```python
import jax
import jax.numpy as jnp
from jax import lax
from jax.sharding import PartitionSpec as P

SESS_DEV = 16
logit_scale = 20.0
epsilon = 1e-06


def passed_along(shard, axis, by):
    length = lax.axis_size(axis)
    return lax.ppermute(shard, axis, [(i, (i + by) % length) for i in range(length)])


def unit_rows(values):
    widened = values.astype(jnp.float32)
    return (
        widened * lax.rsqrt(jnp.sum(widened * widened, axis=-1, keepdims=True) + epsilon)
    ).astype(jnp.bfloat16)


def contract_rows(left_side, right_side):
    return lax.dot_general(
        left_side, right_side, (((1,), (1,)), ((), ())), preferred_element_type=jnp.float32
    )


def contract_first(left_side, right_side):
    return lax.dot_general(
        left_side, right_side, (((0,), (0,)), ((), ())), preferred_element_type=jnp.float32
    )


def on_device(
    spans, span_counts, session_ids, destinations, expert_weight, norm_gain, queries, positives
):
    rows_dev = spans.shape[0]
    hidden_width = spans.shape[1]
    groups = lax.axis_size("dp")
    capacity = (rows_dev - 3 * SESS_DEV) // groups
    received = rows_dev // 4
    live_rows = jnp.arange(rows_dev, dtype=jnp.int32) < span_counts[0]
    expert_ids = jnp.arange(groups, dtype=jnp.int32)
    expert_marks = ((destinations[:, None] == expert_ids[None, :]) & live_rows[:, None]).astype(
        jnp.int32
    )
    before = jnp.cumsum(expert_marks, axis=0) - expert_marks
    slot_index = jnp.where(
        live_rows,
        destinations * capacity + jnp.sum(before * expert_marks, axis=1),
        groups * capacity,
    )
    send_counts = jnp.sum(expert_marks, axis=0)
    send_rows = (
        jnp.zeros((groups * capacity, hidden_width), jnp.bfloat16)
        .at[slot_index]
        .set(spans, mode="drop")
        .reshape(groups, capacity, hidden_width)
    )
    slot_session = (
        jnp.full((groups * capacity,), -1, jnp.int32).at[slot_index].set(session_ids, mode="drop")
    )
    got_rows, got_counts = (
        lax.all_to_all(send_rows, "dp", split_axis=0, concat_axis=0, tiled=True),
        lax.all_to_all(send_counts, "dp", split_axis=0, concat_axis=0, tiled=True),
    )
    slot_rank = jnp.arange(capacity, dtype=jnp.int32)
    valid_slots = slot_rank[None, :] < got_counts[:, None]
    packed_at = jnp.where(
        valid_slots, (jnp.cumsum(got_counts) - got_counts)[:, None] + slot_rank[None, :], received
    ).reshape(groups * capacity)
    packed = (
        jnp.zeros((received, hidden_width), jnp.bfloat16)
        .at[packed_at]
        .set(got_rows.reshape(groups * capacity, hidden_width), mode="drop")
    )
    widened = packed.astype(jnp.float32)
    normed = (
        widened
        * lax.rsqrt(jnp.mean(widened * widened, axis=-1, keepdims=True) + epsilon)
        * norm_gain
    ).astype(jnp.bfloat16)
    embedded = jax.nn.gelu(
        jnp.dot(normed, expert_weight[0], preferred_element_type=jnp.float32), approximate=True
    ).astype(jnp.bfloat16)
    emb_width = embedded.shape[1]
    gather_at = jnp.minimum(packed_at, received - 1)
    outgoing = jnp.where(
        valid_slots.reshape(groups * capacity)[:, None],
        embedded[gather_at],
        jnp.zeros((), jnp.bfloat16),
    ).reshape(groups, capacity, emb_width)
    returned = lax.all_to_all(outgoing, "dp", split_axis=0, concat_axis=0, tiled=True)
    selector = (jnp.arange(SESS_DEV, dtype=jnp.int32)[:, None] == slot_session[None, :]).astype(
        jnp.bfloat16
    )
    pooled = jnp.dot(
        selector, returned.reshape(groups * capacity, emb_width), preferred_element_type=jnp.float32
    )
    doc_unit = unit_rows(pooled)
    query_unit = unit_rows(queries)
    doc_rows = doc_unit.shape[0]
    doc_piece = lax.all_gather(doc_unit, "blk", axis=0, tiled=True)
    piece_rows = doc_piece.shape[0]
    logits = logit_scale * contract_rows(query_unit, doc_piece)
    weights = jnp.exp(logits)
    inside = (positives >= 0) & (positives < piece_rows)
    matches = positives[:, None] == jnp.arange(piece_rows, dtype=jnp.int32)[None, :]
    picked = doc_piece[jnp.clip(positives, 0, piece_rows - 1)].astype(jnp.float32)
    totals = jnp.sum(weights, axis=1)
    numerator = jnp.dot(weights.astype(jnp.bfloat16), doc_piece, preferred_element_type=jnp.float32)
    chosen_logit = jnp.sum(jnp.where(matches, logits, 0.0), axis=1)
    chosen_doc = jnp.where(inside[:, None], picked, 0.0)
    cycle_size = lax.axis_size("blk")
    position = lax.axis_index("blk")

    def backward(step_index, running):
        travelling, accumulated = running
        row_start = (position - step_index) % cycle_size * doc_rows
        logits = logit_scale * contract_rows(query_unit, travelling)
        matches = (positives - row_start)[:, None] == jnp.arange(doc_rows, dtype=jnp.int32)[None, :]
        coefficient = (jnp.exp(logits) / totals[:, None] - matches.astype(jnp.float32)).astype(
            jnp.bfloat16
        )
        accumulated = accumulated + logit_scale * contract_first(coefficient, query_unit)
        travelling = passed_along(travelling, "blk", 1)
        accumulated = passed_along(accumulated, "blk", 1)
        return (travelling, accumulated)

    grad_docs = lax.fori_loop(
        0, cycle_size, backward, (doc_unit, jnp.zeros((doc_rows, emb_width), jnp.float32))
    )[1]
    loss_rows = jnp.log(totals) - chosen_logit
    grad_queries = (logit_scale * (numerator / totals[:, None] - chosen_doc)).astype(jnp.bfloat16)
    return (loss_rows, grad_queries, grad_docs)


def solution(mesh):
    placed = (
        P(("dp", "blk"), None),
        P(("dp", "blk")),
        P(("dp", "blk")),
        P(("dp", "blk")),
        P("dp", None, None),
        P(),
        P(("dp", "blk"), None),
        P(("dp", "blk")),
    )
    return jax.shard_map(
        on_device,
        mesh=mesh,
        in_specs=placed,
        out_specs=(P(("dp", "blk")), P(("dp", "blk"), None), P(("dp", "blk"), None)),
        check_vma=False,
    )
```

profile of v0, /device:TPU:0, one launch (start us, length us, event | category | flops | bytes accessed | tf_op | source)
XLA Modules:
  0.0 356.3 jit_solution(18068380321817378988)
XLA Ops:
  1.3 0.7 fusion.36
  2.0 2.3 reduce-window.18
  4.3 0.3 slice_reduce_fusion
  4.6 0.2 reduce-window.19
  4.7 0.1 add_bitcast_fusion
  4.8 0.8 fusion.38
  5.7 0.7 copy.13
  6.4 5.2 %all-to-all-start = ((s32[8,1,1]{2,1,0:T(1,128)}), s32[8,1,1]{2,1,0:T(1,128)S(1)}, u32[]{:S(2)}, u32[]{:S(2)}) async-start(s32[8,1,1]{2,1,0:T(1,128)} %copy.13), calls=%async_computation | async-start | bytes 8192 | tf_op jit(solution)/shard_map/all_to_all | solution.py:66
  11.5 0.7 compare_select_fusion.2
  12.2 9.7 %scatter_custom_fusion.1 = bf16[1232,1024]{1,0:T(8,128)(2,1)S(1)} fusion(s32[1280]{0:T(1024)S(1)} %compare_select_fusion.2, bf16[1280,1024]{1,0:T(8,128)(2,1)} %param.10, bf16[]{:T(256)} %constant.108.clone.1), kind=kCustom, calls=%fused_computation.41 | custom fusion | bytes 2523648 | tf_op jit(solution)/shard_map/scatter | solution.py:58
  21.9 0.0 copy-start.2
  21.9 1.8 reshape.207
  23.8 0.0 all-to-all-done
  23.8 4.2 %all-to-all-start.1 = ((bf16[8,154,1024]{2,1,0:T(8,128)(2,1)}), bf16[8,154,1024]{2,1,0:T(8,128)(2,1)S(1)}, u32[]{:S(2)}, u32[]{:S(2)}) async-start(bf16[8,154,1024]{2,1,0:T(8,128)(2,1)} %reshape.207), calls=%async_computation.1 | async-start | bytes 5242880 | tf_op jit(solution)/shard_map/all_to_all | solution.py:65
  28.0 0.2 reduce.1
  28.2 0.2 reduce-window.20
  28.4 0.1 add_select_fusion
  28.5 0.1 select_n.86
  28.6 0.1 iota_compare_fusion.7
  28.7 31.5 %all-to-all-done.1 = bf16[8,154,1024]{2,1,0:T(8,128)(2,1)S(1)} async-done(((bf16[8,154,1024]{2,1,0:T(8,128)(2,1)}), bf16[8,154,1024]{2,1,0:T(8,128)(2,1)S(1)}, u32[]{:S(2)}, u32[]{:S(2)}) %all-to-all-start.1) | async-done | bytes 2523168 | tf_op jit(solution)/shard_map/all_to_all | solution.py:65
  60.2 1.8 reshape.246
  62.0 9.5 %scatter_custom_fusion.2 = bf16[320,1024]{1,0:T(8,128)(2,1)S(1)} fusion(s32[1232]{0:T(1024)S(1)} %get-tuple-element.186, bf16[1232,1024]{1,0:T(8,128)(2,1)} %reshape.246, bf16[]{:T(256)} %constant.108.clone.1), kind=kCustom, calls=%fused_computation.46 | custom fusion | bytes 655872 | tf_op jit(solution)/shard_map/scatter | solution.py:76
  71.6 0.2 fusion.24
  71.8 0.0 copy-done.2
  71.8 7.3 %fusion.21 = bf16[320,4096]{1,0:T(8,128)(2,1)S(1)} fusion(bf16[1,1024,4096]{2,1,0:T(8,128)(2,1)} %param.14, bf16[320,1024]{1,0:T(8,128)(2,1)S(1)} %scatter_custom_fusion.2, f32[1024]{0:T(1024)S(1)} %copy-done.2, f32[320]{0:T(512)S(1)} %add_rsqrt_fusion.1), kind=kOutput, calls=%fused_computation.35 | convolution fusion | flops 2697461760 | bytes 11670784 | tf_op jit(solution)/shard_map/dot_general | solution.py:85
  79.1 8.2 %gather_fusion = bf16[1232,4096]{1,0:T(8,128)(2,1)} fusion(bf16[320,4096]{1,0:T(8,128)(2,1)S(1)} %fusion.21, s32[2048]{0:T(1024)S(1)} %pad_clamp_fusion), kind=kCustom, calls=%fused_computation | custom fusion | bytes 20190016 | tf_op jit(solution)/shard_map/gather | solution.py:91
  87.4 12.1 %gather.9 = bf16[8,154,4096]{2,1,0:T(8,128)(2,1)} reshape(bf16[1232,4096]{1,0:T(8,128)(2,1)} %gather_fusion) | data formatting | bytes 20185088 | tf_op jit(solution)/shard_map/gather | solution.py:91
  99.5 10.0 %broadcast_select_fusion = bf16[8,154,4096]{2,1,0:T(8,128)(2,1)} fusion(bf16[8,154,4096]{2,1,0:T(8,128)(2,1)} %gather.9, pred[8,154]{1,0:T(8,128)(4,1)S(1)} %iota_compare_fusion.7), kind=kLoop, calls=%fused_computation.24 | loop fusion | flops 5046272 | bytes 20186320 | tf_op jit(solution)/shard_map/jit(_where)/select_n | solution.py:89
  109.5 5.3 %all-to-all-start.2 = ((bf16[8,154,4096]{2,1,0:T(8,128)(2,1)}), bf16[8,154,4096]{2,1,0:T(8,128)(2,1)}, u32[]{:S(2)}, u32[]{:S(2)}) async-start(bf16[8,154,4096]{2,1,0:T(8,128)(2,1)} %broadcast_select_fusion), calls=%async_computation.2 | async-start | bytes 20971520 | tf_op jit(solution)/shard_map/all_to_all | solution.py:94
  114.8 5.6 %scatter_custom_fusion = s32[1232]{0:T(1024)S(1)} fusion(s32[1280]{0:T(1024)S(1)} %compare_select_fusion.2, s32[1280]{0:T(1024)} %param.12, s32[]{:T(128)} %constant.103.clone.1), kind=kCustom, calls=%fused_computation.82 | custom fusion | bytes 5440 | tf_op jit(solution)/shard_map/scatter | solution.py:62
  120.4 4.6 %fusion.10 = f32[896]{0:T(1024)S(1)} fusion(bf16[896,4096]{1,0:T(8,128)(2,1)} %param.16), kind=kLoop, calls=%fused_computation.21 | loop fusion | flops 11009152 | bytes 7343616 | tf_op jit(solution)/shard_map/reduce_sum | solution.py:19
  125.0 9.0 %fusion.11 = bf16[896,4096]{1,0:T(8,128)(2,1)} fusion(bf16[896,4096]{1,0:T(8,128)(2,1)} %param.16, f32[896]{0:T(1024)S(1)} %add_rsqrt_fusion), kind=kLoop, calls=%fused_computation.22 | loop fusion | flops 11010048 | bytes 14683648 | tf_op jit(solution)/shard_map/convert_element_type | solution.py:20
  134.0 97.3 %all-to-all-done.2 = bf16[8,154,4096]{2,1,0:T(8,128)(2,1)} async-done(((bf16[8,154,4096]{2,1,0:T(8,128)(2,1)}), bf16[8,154,4096]{2,1,0:T(8,128)(2,1)}, u32[]{:S(2)}, u32[]{:S(2)}) %all-to-all-start.2) | async-done | bytes 10092576 | tf_op jit(solution)/shard_map/all_to_all | solution.py:94
  231.3 12.2 %reshape.209 = bf16[1232,4096]{1,0:T(8,128)(2,1)} reshape(bf16[8,154,4096]{2,1,0:T(8,128)(2,1)} %all-to-all-done.2) | data formatting | bytes 20185088 | tf_op jit(solution)/shard_map/reshape | solution.py:99
  243.4 5.5 %multiply_reduce_fusion = (f32[16]{0:T(128)S(1)}, f32[16,4096]{1,0:T(8,128)S(1)}) fusion(bf16[1232,4096]{1,0:T(8,128)(2,1)} %reshape.209, s32[1232]{0:T(1024)S(1)} %scatter_custom_fusion), kind=kOutput, calls=%fused_computation.49 | convolution fusion | flops 161631472 | bytes 10359680 | tf_op jit(solution)/shard_map/dot_general | solution.py:98
  249.0 0.1 multiply_convert_fusion.1
  249.1 16.4 %all_gather.3 = bf16[64,4096]{1,0:T(8,128)(2,1)S(1)} all-gather(bf16[16,4096]{1,0:T(8,128)(2,1)S(1)} %multiply_convert_fusion.1), channel_id=1, replica_groups=mesh['dp'=8,'blk'=4] {'blk'}, dimensions={0}, use_global_device_ids=true | all-gather | bytes 655360 | tf_op jit(solution)/shard_map/all_gather | solution.py:104
  265.5 0.0 copy-done
  265.5 2.4 exponential_reduce_fusion
  267.9 73.3 %while.17 = (s32[]{:T(128)}, bf16[16,4096]{1,0:T(8,128)(2,1)S(1)}, f32[16,4096]{1,0:T(8,128)S(1)}, bf16[896,4096]{1,0:T(8,128)(2,1)}, f32[896]{0:T(1024)S(1)}, /...) while((s32[]{:T(128)}, bf16[16,4096]{1,0:T(8,128)(2,1)S(1)}, ...), condition=%wide.region_14.15_spmd, body=%wide.region_13.14_spmd.sunk | while | flops 235099024 | bytes 9845070 | solution.py:131
  268.0 8.7 %fusion.59 = f32[16,4096]{1,0:T(8,128)S(1)} fusion(f32[16,4096]{1,0:T(8,128)S(1)} %get-tuple-element.261, bf16[896,4096]{1,0:T(8,128)(2,1)} %get-tuple-element.274, bf16[16,4096]{1,0:T(8,128)(2,1)S(1)} %copy.20, s32[896]{0:T(1024)S(1)} %broadcast_subtract_fusion.2, f32[896]{0:T(1024)S(1)} %get-tuple-element.275), kind=kOutput, calls=%fused_computation.6.clone.1 | convolution fusion | flops 235098112 | bytes 8002560 | tf_op jit(solution)/shard_map/while/body/eval_jaxpr/dot_general | solution.py:30
  276.7 0.3 collective-permute-start.1
  277.0 1.0 collective-permute-start
  278.0 8.3 %collective-permute-done = bf16[16,4096]{1,0:T(8,128)(2,1)S(1)} collective-permute-done((bf16[16,4096]{1,0:T(8,128)(2,1)S(1)}, bf16[16,4096]{1,0:T(8,128)(2,1)S(1)}, u32[]{:S(2)}, u32[]{:S(2)}) %collective-permute-start) | collective-permute-done | bytes 131104 | tf_op jit(solution)/shard_map/while/body/eval_jaxpr/ppermute | solution.py:13
  286.3 0.0 collective-permute-done.1
  286.3 8.7 %fusion.59 = f32[16,4096]{1,0:T(8,128)S(1)} fusion(f32[16,4096]{1,0:T(8,128)S(1)} %get-tuple-element.261, bf16[896,4096]{1,0:T(8,128)(2,1)} %get-tuple-element.274, bf16[16,4096]{1,0:T(8,128)(2,1)S(1)} %copy.20, s32[896]{0:T(1024)S(1)} %broadcast_subtract_fusion.2, f32[896]{0:T(1024)S(1)} %get-tuple-element.275), kind=kOutput, calls=%fused_computation.6.clone.1 | convolution fusion | flops 235098112 | bytes 8002560 | tf_op jit(solution)/shard_map/while/body/eval_jaxpr/dot_general | solution.py:30
  295.0 0.0 collective-permute-start.1
  295.0 0.1 collective-permute-start
  295.1 9.5 %collective-permute-done = bf16[16,4096]{1,0:T(8,128)(2,1)S(1)} collective-permute-done((bf16[16,4096]{1,0:T(8,128)(2,1)S(1)}, bf16[16,4096]{1,0:T(8,128)(2,1)S(1)}, u32[]{:S(2)}, u32[]{:S(2)}) %collective-permute-start) | collective-permute-done | bytes 131104 | tf_op jit(solution)/shard_map/while/body/eval_jaxpr/ppermute | solution.py:13
  304.6 0.0 collective-permute-done.1
  304.6 8.7 %fusion.59 = f32[16,4096]{1,0:T(8,128)S(1)} fusion(f32[16,4096]{1,0:T(8,128)S(1)} %get-tuple-element.261, bf16[896,4096]{1,0:T(8,128)(2,1)} %get-tuple-element.274, bf16[16,4096]{1,0:T(8,128)(2,1)S(1)} %copy.20, s32[896]{0:T(1024)S(1)} %broadcast_subtract_fusion.2, f32[896]{0:T(1024)S(1)} %get-tuple-element.275), kind=kOutput, calls=%fused_computation.6.clone.1 | convolution fusion | flops 235098112 | bytes 8002560 | tf_op jit(solution)/shard_map/while/body/eval_jaxpr/dot_general | solution.py:30
  313.3 0.0 collective-permute-start.1
  313.3 0.1 collective-permute-start
  313.4 9.5 %collective-permute-done = bf16[16,4096]{1,0:T(8,128)(2,1)S(1)} collective-permute-done((bf16[16,4096]{1,0:T(8,128)(2,1)S(1)}, bf16[16,4096]{1,0:T(8,128)(2,1)S(1)}, u32[]{:S(2)}, u32[]{:S(2)}) %collective-permute-start) | collective-permute-done | bytes 131104 | tf_op jit(solution)/shard_map/while/body/eval_jaxpr/ppermute | solution.py:13
  322.9 0.0 collective-permute-done.1
  323.0 8.7 %fusion.59 = f32[16,4096]{1,0:T(8,128)S(1)} fusion(f32[16,4096]{1,0:T(8,128)S(1)} %get-tuple-element.261, bf16[896,4096]{1,0:T(8,128)(2,1)} %get-tuple-element.274, bf16[16,4096]{1,0:T(8,128)(2,1)S(1)} %copy.20, s32[896]{0:T(1024)S(1)} %broadcast_subtract_fusion.2, f32[896]{0:T(1024)S(1)} %get-tuple-element.275), kind=kOutput, calls=%fused_computation.6.clone.1 | convolution fusion | flops 235098112 | bytes 8002560 | tf_op jit(solution)/shard_map/while/body/eval_jaxpr/dot_general | solution.py:30
  331.7 0.0 collective-permute-start.1
  331.7 0.1 collective-permute-start
  331.7 9.5 %collective-permute-done = bf16[16,4096]{1,0:T(8,128)(2,1)S(1)} collective-permute-done((bf16[16,4096]{1,0:T(8,128)(2,1)S(1)}, bf16[16,4096]{1,0:T(8,128)(2,1)S(1)}, u32[]{:S(2)}, u32[]{:S(2)}) %collective-permute-start) | collective-permute-done | bytes 131104 | tf_op jit(solution)/shard_map/while/body/eval_jaxpr/ppermute | solution.py:13
  341.2 0.0 collective-permute-done.1
  341.2 6.6 %gather_fusion.1 = bf16[896,4096]{1,0:T(8,128)(2,1)} fusion(bf16[64,4096]{1,0:T(8,128)(2,1)S(1)} %all_gather.3, s32[1024]{0:T(1024)S(1)} %pad_clamp_fusion.1), kind=kCustom, calls=%fused_computation.1 | custom fusion | bytes 14683648 | tf_op jit(solution)/shard_map/gather | solution.py:110
  347.8 0.6 log_subtract_fusion
  348.4 7.2 %multiply_convert_fusion = bf16[896,4096]{1,0:T(8,128)(2,1)} fusion(bf16[896,4096]{1,0:T(8,128)(2,1)} %gather_fusion.1, f32[896]{0:T(1024)S(1)} %get-tuple-element.296, pred[896]{0:T(1024)(128)(4,1)S(1)} %compare_and_fusion, bf16[64,4096]{1,0:T(8,128)(2,1)S(1)} %all_gather.3, f32[896,64]{0,1:T(8,128)S(1)} %get-tuple-element.203), kind=kOutput, calls=%fused_computation.23 | convolution fusion | flops 491839488 | bytes 15438208 | tf_op jit(solution)/shard_map/dot_general | solution.py:112
  355.6 0.7 copy.27
  (23 shorter events, 0.2 us)
Async XLA Ops:
  6.4 17.4 %all-to-all-start = ((s32[8,1,1]{2,1,0:T(1,128)}), s32[8,1,1]{2,1,0:T(1,128)S(1)}, u32[]{:S(2)}, u32[]{:S(2)}) async-start(s32[8,1,1]{2,1,0:T(1,128)} %copy.13), calls=%async_computation | async-start | bytes 8192 | tf_op jit(solution)/shard_map/all_to_all | solution.py:66
  21.9 49.9 %copy-start.2 = (f32[1024]{0:T(1024)S(1)}, f32[1024]{0:T(1024)}, u32[]{:S(2)}) copy-start(f32[1024]{0:T(1024)} %param.15) | copy-start | bytes 12292
  23.8 36.5 %all-to-all-start.1 = ((bf16[8,154,1024]{2,1,0:T(8,128)(2,1)}), bf16[8,154,1024]{2,1,0:T(8,128)(2,1)S(1)}, u32[]{:S(2)}, u32[]{:S(2)}) async-start(bf16[8,154,1024]{2,1,0:T(8,128)(2,1)} %reshape.207), calls=%async_computation.1 | async-start | bytes 5242880 | tf_op jit(solution)/shard_map/all_to_all | solution.py:65
  109.5 10.9 %copy-start.1 = (s32[896]{0:T(1024)S(1)}, s32[896]{0:T(1024)}, u32[]{:S(2)}) copy-start(s32[896]{0:T(1024)} %param.17) | copy-start | bytes 10756
  109.5 121.8 %all-to-all-start.2 = ((bf16[8,154,4096]{2,1,0:T(8,128)(2,1)}), bf16[8,154,4096]{2,1,0:T(8,128)(2,1)}, u32[]{:S(2)}, u32[]{:S(2)}) async-start(bf16[8,154,4096]{2,1,0:T(8,128)(2,1)} %broadcast_select_fusion), calls=%async_computation.2 | async-start | bytes 20971520 | tf_op jit(solution)/shard_map/all_to_all | solution.py:94
  243.4 22.1 %copy-start = (bf16[896,4096]{1,0:T(8,128)(2,1)S(1)}, bf16[896,4096]{1,0:T(8,128)(2,1)}, u32[]{:S(2)}) copy-start(bf16[896,4096]{1,0:T(8,128)(2,1)} %fusion.11) | copy-start | bytes 22020100
  276.7 9.6 %collective-permute-start.1 = (f32[16,4096]{1,0:T(8,128)S(1)}, f32[16,4096]{1,0:T(8,128)S(1)}, u32[]{:S(2)}, u32[]{:S(2)}) collective-permute-start(f32[16,4096]{1,0:T(8,128)S(1)} %fusion.59), channel_id=1, source_target_pairs={{0,1},{1,2},{2,3},{3,0},{4,5},{5,6},{6,7},{7,4},{8,9},{9,10},{10,1... | collective-permute-start | bytes 786440 | tf_op jit(solution)/shard_map/while/body/eval_jaxpr/ppermute | solution.py:13
  277.0 9.2 %collective-permute-start = (bf16[16,4096]{1,0:T(8,128)(2,1)S(1)}, bf16[16,4096]{1,0:T(8,128)(2,1)S(1)}, u32[]{:S(2)}, u32[]{:S(2)}) collective-permute-start(bf16[16,4096]{1,0:T(8,128)(2,1)S(1)} %copy.20), channel_id=1, source_target_pairs={{0,1},{1,2},{2,3},{3,0},{4,5},{5,6},{6,7},{7,4},{8,9},{9,10},{10,1... | collective-permute-start | bytes 393224 | tf_op jit(solution)/shard_map/while/body/eval_jaxpr/ppermute | solution.py:13
  295.0 9.6 %collective-permute-start.1 = (f32[16,4096]{1,0:T(8,128)S(1)}, f32[16,4096]{1,0:T(8,128)S(1)}, u32[]{:S(2)}, u32[]{:S(2)}) collective-permute-start(f32[16,4096]{1,0:T(8,128)S(1)} %fusion.59), channel_id=1, source_target_pairs={{0,1},{1,2},{2,3},{3,0},{4,5},{5,6},{6,7},{7,4},{8,9},{9,10},{10,1... | collective-permute-start | bytes 786440 | tf_op jit(solution)/shard_map/while/body/eval_jaxpr/ppermute | solution.py:13
  295.0 9.6 %collective-permute-start = (bf16[16,4096]{1,0:T(8,128)(2,1)S(1)}, bf16[16,4096]{1,0:T(8,128)(2,1)S(1)}, u32[]{:S(2)}, u32[]{:S(2)}) collective-permute-start(bf16[16,4096]{1,0:T(8,128)(2,1)S(1)} %copy.20), channel_id=1, source_target_pairs={{0,1},{1,2},{2,3},{3,0},{4,5},{5,6},{6,7},{7,4},{8,9},{9,10},{10,1... | collective-permute-start | bytes 393224 | tf_op jit(solution)/shard_map/while/body/eval_jaxpr/ppermute | solution.py:13
  313.3 9.6 %collective-permute-start.1 = (f32[16,4096]{1,0:T(8,128)S(1)}, f32[16,4096]{1,0:T(8,128)S(1)}, u32[]{:S(2)}, u32[]{:S(2)}) collective-permute-start(f32[16,4096]{1,0:T(8,128)S(1)} %fusion.59), channel_id=1, source_target_pairs={{0,1},{1,2},{2,3},{3,0},{4,5},{5,6},{6,7},{7,4},{8,9},{9,10},{10,1... | collective-permute-start | bytes 786440 | tf_op jit(solution)/shard_map/while/body/eval_jaxpr/ppermute | solution.py:13
  313.3 9.6 %collective-permute-start = (bf16[16,4096]{1,0:T(8,128)(2,1)S(1)}, bf16[16,4096]{1,0:T(8,128)(2,1)S(1)}, u32[]{:S(2)}, u32[]{:S(2)}) collective-permute-start(bf16[16,4096]{1,0:T(8,128)(2,1)S(1)} %copy.20), channel_id=1, source_target_pairs={{0,1},{1,2},{2,3},{3,0},{4,5},{5,6},{6,7},{7,4},{8,9},{9,10},{10,1... | collective-permute-start | bytes 393224 | tf_op jit(solution)/shard_map/while/body/eval_jaxpr/ppermute | solution.py:13
  331.7 9.6 %collective-permute-start.1 = (f32[16,4096]{1,0:T(8,128)S(1)}, f32[16,4096]{1,0:T(8,128)S(1)}, u32[]{:S(2)}, u32[]{:S(2)}) collective-permute-start(f32[16,4096]{1,0:T(8,128)S(1)} %fusion.59), channel_id=1, source_target_pairs={{0,1},{1,2},{2,3},{3,0},{4,5},{5,6},{6,7},{7,4},{8,9},{9,10},{10,1... | collective-permute-start | bytes 786440 | tf_op jit(solution)/shard_map/while/body/eval_jaxpr/ppermute | solution.py:13
  331.7 9.6 %collective-permute-start = (bf16[16,4096]{1,0:T(8,128)(2,1)S(1)}, bf16[16,4096]{1,0:T(8,128)(2,1)S(1)}, u32[]{:S(2)}, u32[]{:S(2)}) collective-permute-start(bf16[16,4096]{1,0:T(8,128)(2,1)S(1)} %copy.20), channel_id=1, source_target_pairs={{0,1},{1,2},{2,3},{3,0},{4,5},{5,6},{6,7},{7,4},{8,9},{9,10},{10,1... | collective-permute-start | bytes 393224 | tf_op jit(solution)/shard_map/while/body/eval_jaxpr/ppermute | solution.py:13
where the time goes:
time: 357 us; the launch traced here: 356 us
  waiting for transfers between devices  166 us (46%)
  local copies, waits for them, and re-layouts  69.4 us (19%)
  matrix products  57.2 us (16%)
  other arithmetic  29.9 us (8%)
  blocking collectives  16.4 us (5%)
  starting transfers between devices  16.1 us (5%)
    all_to_all x1, waiting for transfers between devices, on_device(): lax.all_to_all(outgoing, 'dp', split_axis=0, concat_axis=0, tiled=True)  97.3 us
    ppermute x8, waiting for transfers between devices, passed_along(): lax.ppermute(shard, axis, [(i, (i + by) % length) for i in range(length)])  36.8 us
    dot_general x4, matrix products, contract_first(): lax.dot_general(left_side, right_side, (((0,), (0,)), ((), ())), preferre...  34.8 us
    all_to_all x1, waiting for transfers between devices, on_device(): lax.all_to_all(send_rows, 'dp', split_axis=0, concat_axis=0, tiled=True)  31.5 us
    gather x2, local copies, waits for them, and re-layouts, on_device(): embedded[gather_at]  20.4 us
    all_gather x1, blocking collectives, on_device(): doc_piece = lax.all_gather(doc_unit, 'blk', axis=0, tiled=True)  16.4 us
    reshape x1, local copies, waits for them, and re-layouts, on_device(): returned.reshape(groups * capacity, emb_width)  12.2 us
    select_n x1, other arithmetic, on_device(): jnp.where(valid_slots.reshape(groups * capacity)[:, None], embedded[gathe...  9.97 us
  transfers between devices with their start and end apart: 11, of which 6 were waited for; matrix products, arithmetic and copies ran while one was open for 9% of the time, Pallas kernels for 0%

commit v1 on v0

--- a/solution.py
+++ b/solution.py
@@ -101,7 +101,12 @@
     doc_unit = unit_rows(pooled)
     query_unit = unit_rows(queries)
     doc_rows = doc_unit.shape[0]
-    doc_piece = lax.all_gather(doc_unit, "blk", axis=0, tiled=True)
+    ring = [doc_unit]
+    for hop in range(3):
+        ring.append(lax.ppermute(ring[-1], "blk", [(dev, (dev + 1) % 4) for dev in range(4)]))
+    doc_piece = jnp.roll(
+        jnp.concatenate(ring[::-1], axis=0), (lax.axis_index("blk") + 1) * ring[0].shape[0], axis=0
+    )
     piece_rows = doc_piece.shape[0]
     logits = logit_scale * contract_rows(query_unit, doc_piece)
     weights = jnp.exp(logits)

time: 357 us -> 380 us (1.064)
  waiting for transfers between devices: 166 us -> 187 us
  blocking collectives: 16.4 us -> 0 us
  other arithmetic: 29.9 us -> 41.4 us
    all_gather x1 -> x0, blocking collectives: 16.4 us -> none  [on_device(): doc_piece = lax.all_gather(doc_unit, 'blk', axis=0, tiled=True)]
    convert_element_type x0 -> x1, other arithmetic: none -> 11.4 us  [on_device(): (logit_scale * (numerator / totals[:, None] - chosen_doc)).astype(jnp.bfl...]
    ppermute x0 -> x3, waiting for transfers between devices: none -> 11.1 us  [on_device(): lax.ppermute(ring[-1], 'blk', [(dev, (dev + 1) % 4) for dev in range(4)])]
    all_to_all x1, waiting for transfers between devices: 97.3 us -> 106 us  [on_device(): lax.all_to_all(outgoing, 'dp', split_axis=0, concat_axis=0, tiled=True)]
    ppermute x0 -> x3, starting transfers between devices: none -> 4.19 us  [on_device(): lax.ppermute(ring[-1], 'blk', [(dev, (dev + 1) % 4) for dev in range(4)])]
  transfers between devices with their start and end apart: 11 -> 14, of which waited for: 6 -> 8; matrix products, arithmetic and copies ran while one was open for 9% -> 8% of each run, Pallas kernels for 0% -> 0%
where the time goes in v1:
time: 380 us; the launch traced here: 379 us
  waiting for transfers between devices  187 us (49%)
  local copies, waits for them, and re-layouts  69.5 us (18%)
  matrix products  60.3 us (16%)
  other arithmetic  41.4 us (11%)
  starting transfers between devices  19.2 us (5%)
    all_to_all x1, waiting for transfers between devices, on_device(): lax.all_to_all(outgoing, 'dp', split_axis=0, concat_axis=0, tiled=True)  106 us
    ppermute x8, waiting for transfers between devices, passed_along(): lax.ppermute(shard, axis, [(i, (i + by) % length) for i in range(length)])  37.8 us
    dot_general x4, matrix products, contract_first(): lax.dot_general(left_side, right_side, (((0,), (0,)), ((), ())), preferre...  34.8 us
    all_to_all x1, waiting for transfers between devices, on_device(): lax.all_to_all(send_rows, 'dp', split_axis=0, concat_axis=0, tiled=True)  31.5 us
    gather x2, local copies, waits for them, and re-layouts, on_device(): embedded[gather_at]  20.4 us
    reshape x1, local copies, waits for them, and re-layouts, on_device(): returned.reshape(groups * capacity, emb_width)  12.2 us
    convert_element_type x1, other arithmetic, on_device(): (logit_scale * (numerator / totals[:, None] - chosen_doc)).astype(jnp.bfl...  11.4 us
    ppermute x3, waiting for transfers between devices, on_device(): lax.ppermute(ring[-1], 'blk', [(dev, (dev + 1) % 4) for dev in range(4)])  11.1 us
  transfers between devices with their start and end apart: 14, of which 8 were waited for; matrix products, arithmetic and copies ran while one was open for 8% of the time, Pallas kernels for 0%

profile of v1, /device:TPU:0, one launch (start us, length us, event | category | flops | bytes accessed | tf_op | source)
XLA Modules:
  0.0 378.8 jit_solution(3239324119281498882)
XLA Ops:
  1.3 0.7 fusion.37
  2.0 2.3 reduce-window.18
  4.3 0.3 slice_reduce_fusion
  4.6 0.2 reduce-window.19
  4.7 0.1 add_bitcast_fusion
  4.8 0.8 fusion.39
  5.7 0.7 copy.13
  6.4 5.2 %all-to-all-start = ((s32[8,1,1]{2,1,0:T(1,128)}), s32[8,1,1]{2,1,0:T(1,128)S(1)}, u32[]{:S(2)}, u32[]{:S(2)}) async-start(s32[8,1,1]{2,1,0:T(1,128)} %copy.13), calls=%async_computation | async-start | bytes 8192 | tf_op jit(solution)/shard_map/all_to_all | solution.py:66
  11.5 0.7 compare_select_fusion.2
  12.2 9.7 %scatter_custom_fusion.1 = bf16[1232,1024]{1,0:T(8,128)(2,1)S(1)} fusion(s32[1280]{0:T(1024)S(1)} %compare_select_fusion.2, bf16[1280,1024]{1,0:T(8,128)(2,1)} %param.10, bf16[]{:T(256)} %constant.128.clone.1), kind=kCustom, calls=%fused_computation.41 | custom fusion | bytes 2523648 | tf_op jit(solution)/shard_map/scatter | solution.py:58
  21.9 0.0 copy-start.1
  21.9 1.8 reshape.207
  23.8 4.2 %all-to-all-start.1 = ((bf16[8,154,1024]{2,1,0:T(8,128)(2,1)}), bf16[8,154,1024]{2,1,0:T(8,128)(2,1)S(1)}, u32[]{:S(2)}, u32[]{:S(2)}) async-start(bf16[8,154,1024]{2,1,0:T(8,128)(2,1)} %reshape.207), calls=%async_computation.1 | async-start | bytes 5242880 | tf_op jit(solution)/shard_map/all_to_all | solution.py:65
  28.0 0.2 reduce.1
  28.2 0.2 reduce-window.20
  28.4 0.1 add_select_fusion
  28.5 0.1 select_n.98
  28.6 0.1 iota_compare_fusion.7
  28.7 31.5 %all-to-all-done.1 = bf16[8,154,1024]{2,1,0:T(8,128)(2,1)S(1)} async-done(((bf16[8,154,1024]{2,1,0:T(8,128)(2,1)}), bf16[8,154,1024]{2,1,0:T(8,128)(2,1)S(1)}, u32[]{:S(2)}, u32[]{:S(2)}) %all-to-all-start.1) | async-done | bytes 2523168 | tf_op jit(solution)/shard_map/all_to_all | solution.py:65
  60.2 1.8 reshape.246
  62.0 9.5 %scatter_custom_fusion.2 = bf16[320,1024]{1,0:T(8,128)(2,1)S(1)} fusion(s32[1232]{0:T(1024)S(1)} %get-tuple-element.186, bf16[1232,1024]{1,0:T(8,128)(2,1)} %reshape.246, bf16[]{:T(256)} %constant.128.clone.1), kind=kCustom, calls=%fused_computation.46 | custom fusion | bytes 655872 | tf_op jit(solution)/shard_map/scatter | solution.py:76
  71.6 0.2 fusion.24
  71.8 7.3 %fusion.21 = bf16[320,4096]{1,0:T(8,128)(2,1)S(1)} fusion(bf16[1,1024,4096]{2,1,0:T(8,128)(2,1)} %param.14, bf16[320,1024]{1,0:T(8,128)(2,1)S(1)} %scatter_custom_fusion.2, f32[1024]{0:T(1024)S(1)} %copy-done.1, f32[320]{0:T(512)S(1)} %add_rsqrt_fusion.1), kind=kOutput, calls=%fused_computation.35 | convolution fusion | flops 2697461760 | bytes 11670784 | tf_op jit(solution)/shard_map/dot_general | solution.py:85
  79.1 8.2 %gather_fusion = bf16[1232,4096]{1,0:T(8,128)(2,1)} fusion(bf16[320,4096]{1,0:T(8,128)(2,1)S(1)} %fusion.21, s32[2048]{0:T(1024)S(1)} %pad_clamp_fusion), kind=kCustom, calls=%fused_computation | custom fusion | bytes 20190016 | tf_op jit(solution)/shard_map/gather | solution.py:91
  87.4 12.1 %gather.9 = bf16[8,154,4096]{2,1,0:T(8,128)(2,1)} reshape(bf16[1232,4096]{1,0:T(8,128)(2,1)} %gather_fusion) | data formatting | bytes 20185088 | tf_op jit(solution)/shard_map/gather | solution.py:91
  99.5 10.0 %broadcast_select_fusion = bf16[8,154,4096]{2,1,0:T(8,128)(2,1)} fusion(bf16[8,154,4096]{2,1,0:T(8,128)(2,1)} %gather.9, pred[8,154]{1,0:T(8,128)(4,1)S(1)} %iota_compare_fusion.7), kind=kLoop, calls=%fused_computation.24 | loop fusion | flops 5046272 | bytes 20186320 | tf_op jit(solution)/shard_map/jit(_where)/select_n | solution.py:89
  109.5 5.1 %all-to-all-start.2 = ((bf16[8,154,4096]{2,1,0:T(8,128)(2,1)}), bf16[8,154,4096]{2,1,0:T(8,128)(2,1)}, u32[]{:S(2)}, u32[]{:S(2)}) async-start(bf16[8,154,4096]{2,1,0:T(8,128)(2,1)} %broadcast_select_fusion), calls=%async_computation.2 | async-start | bytes 20971520 | tf_op jit(solution)/shard_map/all_to_all | solution.py:94
  114.6 5.6 %scatter_custom_fusion = s32[1232]{0:T(1024)S(1)} fusion(s32[1280]{0:T(1024)S(1)} %compare_select_fusion.2, s32[1280]{0:T(1024)} %param.12, s32[]{:T(128)} %constant.123.clone.1), kind=kCustom, calls=%fused_computation.91 | custom fusion | bytes 5440 | tf_op jit(solution)/shard_map/scatter | solution.py:62
  120.3 4.6 %fusion.10 = f32[896]{0:T(1024)S(1)} fusion(bf16[896,4096]{1,0:T(8,128)(2,1)} %param.16), kind=kLoop, calls=%fused_computation.21 | loop fusion | flops 11009152 | bytes 7343616 | tf_op jit(solution)/shard_map/reduce_sum | solution.py:19
  124.8 106.3 %all-to-all-done.2 = bf16[8,154,4096]{2,1,0:T(8,128)(2,1)} async-done(((bf16[8,154,4096]{2,1,0:T(8,128)(2,1)}), bf16[8,154,4096]{2,1,0:T(8,128)(2,1)}, u32[]{:S(2)}, u32[]{:S(2)}) %all-to-all-start.2) | async-done | bytes 10092576 | tf_op jit(solution)/shard_map/all_to_all | solution.py:94
  231.2 12.2 %reshape.209 = bf16[1232,4096]{1,0:T(8,128)(2,1)} reshape(bf16[8,154,4096]{2,1,0:T(8,128)(2,1)} %all-to-all-done.2) | data formatting | bytes 20185088 | tf_op jit(solution)/shard_map/reshape | solution.py:99
  243.3 5.4 %multiply_reduce_fusion = (f32[16]{0:T(128)S(1)}, f32[16,4096]{1,0:T(8,128)S(1)}) fusion(bf16[1232,4096]{1,0:T(8,128)(2,1)} %reshape.209, s32[1232]{0:T(1024)S(1)} %scatter_custom_fusion), kind=kOutput, calls=%fused_computation.49 | convolution fusion | flops 161631472 | bytes 10359680 | tf_op jit(solution)/shard_map/dot_general | solution.py:98
  248.7 0.1 multiply_convert_fusion.1
  248.8 0.0 copy-start
  248.8 1.6 collective-permute-start.2
  250.4 8.9 %fusion.11 = bf16[896,4096]{1,0:T(8,128)(2,1)} fusion(bf16[896,4096]{1,0:T(8,128)(2,1)} %param.16, f32[896]{0:T(1024)S(1)} %add_rsqrt_fusion), kind=kLoop, calls=%fused_computation.22 | loop fusion | flops 11010048 | bytes 14683648 | tf_op jit(solution)/shard_map/convert_element_type | solution.py:20
  259.4 1.6 collective-permute-start.3
  261.0 5.3 %collective-permute-done.3 = bf16[16,4096]{1,0:T(8,128)(2,1)S(1)} collective-permute-done((bf16[16,4096]{1,0:T(8,128)(2,1)S(1)}, bf16[16,4096]{1,0:T(8,128)(2,1)S(1)}, u32[]{:S(2)}, u32[]{:S(2)}) %collective-permute-start.3) | collective-permute-done | bytes 131104 | tf_op jit(solution)/shard_map/ppermute | solution.py:106
  266.3 1.0 collective-permute-start.4
  267.3 5.8 %collective-permute-done.4 = bf16[16,4096]{1,0:T(8,128)(2,1)S(1)} collective-permute-done((bf16[16,4096]{1,0:T(8,128)(2,1)S(1)}, bf16[16,4096]{1,0:T(8,128)(2,1)S(1)}, u32[]{:S(2)}, u32[]{:S(2)}) %collective-permute-start.4) | collective-permute-done | bytes 131104 | tf_op jit(solution)/shard_map/ppermute | solution.py:106
  273.1 0.1 constant_dynamic-update-slice_fusion.4
  273.3 0.1 constant_dynamic-update-slice_fusion
  273.4 5.4 %exponential_reduce_fusion = (f32[896]{0:T(1024)S(1)}, f32[896]{0:T(1024)S(1)}, f32[896,64]{0,1:T(8,128)S(1)}) fusion(s32[896]{0:T(1024)S(1)} %copy-done, bf16[896,4096]{1,0:T(8,128)(2,1)} %fusion.11, bf16[64,4096]{1,0:T(8,128)(2,1)S(1)} %constant_dynamic-slice_fusion), kind=kOutput, calls=%fused_computation.53 | convolution fusion | flops 470046976 | bytes 8104448 | tf_op jit(solution)/shard_map/dot_general | solution.py:24
  278.9 73.3 %while.17 = (s32[]{:T(128)}, bf16[16,4096]{1,0:T(8,128)(2,1)S(1)}, f32[16,4096]{1,0:T(8,128)S(1)}, bf16[896,4096]{1,0:T(8,128)(2,1)}, f32[896]{0:T(1024)S(1)}, /...) while((s32[]{:T(128)}, bf16[16,4096]{1,0:T(8,128)(2,1)S(1)}, ...), condition=%wide.region_14.15_spmd, body=%wide.region_13.14_spmd.sunk | while | flops 235099024 | bytes 9845070 | solution.py:136
  278.9 8.7 %fusion.60 = f32[16,4096]{1,0:T(8,128)S(1)} fusion(f32[16,4096]{1,0:T(8,128)S(1)} %get-tuple-element.261, bf16[896,4096]{1,0:T(8,128)(2,1)} %get-tuple-element.274, bf16[16,4096]{1,0:T(8,128)(2,1)S(1)} %copy.27, s32[896]{0:T(1024)S(1)} %broadcast_subtract_fusion.2, f32[896]{0:T(1024)S(1)} %get-tuple-element.275), kind=kOutput, calls=%fused_computation.6.clone.1 | convolution fusion | flops 235098112 | bytes 8002560 | tf_op jit(solution)/shard_map/while/body/eval_jaxpr/dot_general | solution.py:30
  287.6 0.3 collective-permute-start
  287.9 9.3 %collective-permute-done = bf16[16,4096]{1,0:T(8,128)(2,1)S(1)} collective-permute-done((bf16[16,4096]{1,0:T(8,128)(2,1)S(1)}, bf16[16,4096]{1,0:T(8,128)(2,1)S(1)}, u32[]{:S(2)}, u32[]{:S(2)}) %collective-permute-start) | collective-permute-done | bytes 131104 | tf_op jit(solution)/shard_map/while/body/eval_jaxpr/ppermute | solution.py:13
  297.2 0.0 collective-permute-done.1
  297.3 8.7 %fusion.60 = f32[16,4096]{1,0:T(8,128)S(1)} fusion(f32[16,4096]{1,0:T(8,128)S(1)} %get-tuple-element.261, bf16[896,4096]{1,0:T(8,128)(2,1)} %get-tuple-element.274, bf16[16,4096]{1,0:T(8,128)(2,1)S(1)} %copy.27, s32[896]{0:T(1024)S(1)} %broadcast_subtract_fusion.2, f32[896]{0:T(1024)S(1)} %get-tuple-element.275), kind=kOutput, calls=%fused_computation.6.clone.1 | convolution fusion | flops 235098112 | bytes 8002560 | tf_op jit(solution)/shard_map/while/body/eval_jaxpr/dot_general | solution.py:30
  306.0 0.0 collective-permute-start.1
  306.0 0.1 collective-permute-start
  306.0 9.5 %collective-permute-done = bf16[16,4096]{1,0:T(8,128)(2,1)S(1)} collective-permute-done((bf16[16,4096]{1,0:T(8,128)(2,1)S(1)}, bf16[16,4096]{1,0:T(8,128)(2,1)S(1)}, u32[]{:S(2)}, u32[]{:S(2)}) %collective-permute-start) | collective-permute-done | bytes 131104 | tf_op jit(solution)/shard_map/while/body/eval_jaxpr/ppermute | solution.py:13
  315.6 8.7 %fusion.60 = f32[16,4096]{1,0:T(8,128)S(1)} fusion(f32[16,4096]{1,0:T(8,128)S(1)} %get-tuple-element.261, bf16[896,4096]{1,0:T(8,128)(2,1)} %get-tuple-element.274, bf16[16,4096]{1,0:T(8,128)(2,1)S(1)} %copy.27, s32[896]{0:T(1024)S(1)} %broadcast_subtract_fusion.2, f32[896]{0:T(1024)S(1)} %get-tuple-element.275), kind=kOutput, calls=%fused_computation.6.clone.1 | convolution fusion | flops 235098112 | bytes 8002560 | tf_op jit(solution)/shard_map/while/body/eval_jaxpr/dot_general | solution.py:30
  324.3 0.0 collective-permute-start.1
  324.3 0.1 collective-permute-start
  324.3 9.5 %collective-permute-done = bf16[16,4096]{1,0:T(8,128)(2,1)S(1)} collective-permute-done((bf16[16,4096]{1,0:T(8,128)(2,1)S(1)}, bf16[16,4096]{1,0:T(8,128)(2,1)S(1)}, u32[]{:S(2)}, u32[]{:S(2)}) %collective-permute-start) | collective-permute-done | bytes 131104 | tf_op jit(solution)/shard_map/while/body/eval_jaxpr/ppermute | solution.py:13
  333.9 8.7 %fusion.60 = f32[16,4096]{1,0:T(8,128)S(1)} fusion(f32[16,4096]{1,0:T(8,128)S(1)} %get-tuple-element.261, bf16[896,4096]{1,0:T(8,128)(2,1)} %get-tuple-element.274, bf16[16,4096]{1,0:T(8,128)(2,1)S(1)} %copy.27, s32[896]{0:T(1024)S(1)} %broadcast_subtract_fusion.2, f32[896]{0:T(1024)S(1)} %get-tuple-element.275), kind=kOutput, calls=%fused_computation.6.clone.1 | convolution fusion | flops 235098112 | bytes 8002560 | tf_op jit(solution)/shard_map/while/body/eval_jaxpr/dot_general | solution.py:30
  342.6 0.1 collective-permute-start
  342.7 9.5 %collective-permute-done = bf16[16,4096]{1,0:T(8,128)(2,1)S(1)} collective-permute-done((bf16[16,4096]{1,0:T(8,128)(2,1)S(1)}, bf16[16,4096]{1,0:T(8,128)(2,1)S(1)}, u32[]{:S(2)}, u32[]{:S(2)}) %collective-permute-start) | collective-permute-done | bytes 131104 | tf_op jit(solution)/shard_map/while/body/eval_jaxpr/ppermute | solution.py:13
  352.2 7.3 %fusion.34 = f32[896,4096]{1,0:T(8,128)} fusion(bf16[64,4096]{1,0:T(8,128)(2,1)S(1)} %constant_dynamic-slice_fusion, f32[896,64]{0,1:T(8,128)S(1)} %get-tuple-element.203), kind=kOutput, calls=%fused_computation.54 | convolution fusion | flops 469819392 | bytes 15433728 | tf_op jit(solution)/shard_map/dot_general | solution.py:117
  359.5 6.6 %gather_fusion.1 = bf16[896,4096]{1,0:T(8,128)(2,1)} fusion(bf16[64,4096]{1,0:T(8,128)(2,1)S(1)} %constant_dynamic-slice_fusion, s32[1024]{0:T(1024)S(1)} %pad_clamp_fusion.1), kind=kCustom, calls=%fused_computation.1 | custom fusion | bytes 14683648 | tf_op jit(solution)/shard_map/gather | solution.py:115
  366.1 0.6 log_subtract_fusion
  366.7 11.4 %multiply_convert_fusion = bf16[896,4096]{1,0:T(8,128)(2,1)} fusion(bf16[896,4096]{1,0:T(8,128)(2,1)} %gather_fusion.1, f32[896,4096]{1,0:T(8,128)} %fusion.34, f32[896]{0:T(1024)S(1)} %get-tuple-element.302, pred[896]{0:T(1024)(128)(4,1)S(1)} %compare_and_fusion), kind=kLoop, calls=%fused_computation.23 | loop fusion | flops 22020096 | bytes 29364608 | tf_op jit(solution)/shard_map/convert_element_type | solution.py:140
  378.1 0.7 copy.34
  (36 shorter events, 0.3 us)
Async XLA Ops:
  6.4 17.4 %all-to-all-start = ((s32[8,1,1]{2,1,0:T(1,128)}), s32[8,1,1]{2,1,0:T(1,128)S(1)}, u32[]{:S(2)}, u32[]{:S(2)}) async-start(s32[8,1,1]{2,1,0:T(1,128)} %copy.13), calls=%async_computation | async-start | bytes 8192 | tf_op jit(solution)/shard_map/all_to_all | solution.py:66
  21.9 49.9 %copy-start.1 = (f32[1024]{0:T(1024)S(1)}, f32[1024]{0:T(1024)}, u32[]{:S(2)}) copy-start(f32[1024]{0:T(1024)} %param.15) | copy-start | bytes 12292
  23.8 36.5 %all-to-all-start.1 = ((bf16[8,154,1024]{2,1,0:T(8,128)(2,1)}), bf16[8,154,1024]{2,1,0:T(8,128)(2,1)S(1)}, u32[]{:S(2)}, u32[]{:S(2)}) async-start(bf16[8,154,1024]{2,1,0:T(8,128)(2,1)} %reshape.207), calls=%async_computation.1 | async-start | bytes 5242880 | tf_op jit(solution)/shard_map/all_to_all | solution.py:65
  109.5 121.7 %all-to-all-start.2 = ((bf16[8,154,4096]{2,1,0:T(8,128)(2,1)}), bf16[8,154,4096]{2,1,0:T(8,128)(2,1)}, u32[]{:S(2)}, u32[]{:S(2)}) async-start(bf16[8,154,4096]{2,1,0:T(8,128)(2,1)} %broadcast_select_fusion), calls=%async_computation.2 | async-start | bytes 20971520 | tf_op jit(solution)/shard_map/all_to_all | solution.py:94
  248.8 12.2 %copy-start = (s32[896]{0:T(1024)S(1)}, s32[896]{0:T(1024)}, u32[]{:S(2)}) copy-start(s32[896]{0:T(1024)} %param.17) | copy-start | bytes 10756
  248.8 10.6 %collective-permute-start.2 = (bf16[16,4096]{1,0:T(8,128)(2,1)S(1)}, bf16[16,4096]{1,0:T(8,128)(2,1)S(1)}, u32[]{:S(2)}, u32[]{:S(2)}) collective-permute-start(bf16[16,4096]{1,0:T(8,128)(2,1)S(1)} %multiply_convert_fusion.1), channel_id=1, source_target_pairs={{0,1},{1,2},{2,3},{3,0},{4,5},{5,6},{6,7},{7,4},{8,9},{9,10},{10,1... | collective-permute-start | bytes 393224 | tf_op jit(solution)/shard_map/ppermute | solution.py:106
  259.4 6.9 %collective-permute-start.3 = (bf16[16,4096]{1,0:T(8,128)(2,1)S(1)}, bf16[16,4096]{1,0:T(8,128)(2,1)S(1)}, u32[]{:S(2)}, u32[]{:S(2)}) collective-permute-start(bf16[16,4096]{1,0:T(8,128)(2,1)S(1)} %collective-permute-done.2), channel_id=1, source_target_pairs={{0,1},{1,2},{2,3},{3,0},{4,5},{5,6},{6,7},{7,4},{8,9},{9,10},{10,1... | collective-permute-start | bytes 393224 | tf_op jit(solution)/shard_map/ppermute | solution.py:106
  266.3 6.8 %collective-permute-start.4 = (bf16[16,4096]{1,0:T(8,128)(2,1)S(1)}, bf16[16,4096]{1,0:T(8,128)(2,1)S(1)}, u32[]{:S(2)}, u32[]{:S(2)}) collective-permute-start(bf16[16,4096]{1,0:T(8,128)(2,1)S(1)} %collective-permute-done.3), channel_id=1, source_target_pairs={{0,1},{1,2},{2,3},{3,0},{4,5},{5,6},{6,7},{7,4},{8,9},{9,10},{10,1... | collective-permute-start | bytes 393224 | tf_op jit(solution)/shard_map/ppermute | solution.py:106
  287.6 9.6 %collective-permute-start.1 = (f32[16,4096]{1,0:T(8,128)S(1)}, f32[16,4096]{1,0:T(8,128)S(1)}, u32[]{:S(2)}, u32[]{:S(2)}) collective-permute-start(f32[16,4096]{1,0:T(8,128)S(1)} %fusion.60), channel_id=1, source_target_pairs={{0,1},{1,2},{2,3},{3,0},{4,5},{5,6},{6,7},{7,4},{8,9},{9,10},{10,1... | collective-permute-start | bytes 786440 | tf_op jit(solution)/shard_map/while/body/eval_jaxpr/ppermute | solution.py:13
  287.6 9.6 %collective-permute-start = (bf16[16,4096]{1,0:T(8,128)(2,1)S(1)}, bf16[16,4096]{1,0:T(8,128)(2,1)S(1)}, u32[]{:S(2)}, u32[]{:S(2)}) collective-permute-start(bf16[16,4096]{1,0:T(8,128)(2,1)S(1)} %copy.27), channel_id=1, source_target_pairs={{0,1},{1,2},{2,3},{3,0},{4,5},{5,6},{6,7},{7,4},{8,9},{9,10},{10,1... | collective-permute-start | bytes 393224 | tf_op jit(solution)/shard_map/while/body/eval_jaxpr/ppermute | solution.py:13
  306.0 9.6 %collective-permute-start.1 = (f32[16,4096]{1,0:T(8,128)S(1)}, f32[16,4096]{1,0:T(8,128)S(1)}, u32[]{:S(2)}, u32[]{:S(2)}) collective-permute-start(f32[16,4096]{1,0:T(8,128)S(1)} %fusion.60), channel_id=1, source_target_pairs={{0,1},{1,2},{2,3},{3,0},{4,5},{5,6},{6,7},{7,4},{8,9},{9,10},{10,1... | collective-permute-start | bytes 786440 | tf_op jit(solution)/shard_map/while/body/eval_jaxpr/ppermute | solution.py:13
  306.0 9.6 %collective-permute-start = (bf16[16,4096]{1,0:T(8,128)(2,1)S(1)}, bf16[16,4096]{1,0:T(8,128)(2,1)S(1)}, u32[]{:S(2)}, u32[]{:S(2)}) collective-permute-start(bf16[16,4096]{1,0:T(8,128)(2,1)S(1)} %copy.27), channel_id=1, source_target_pairs={{0,1},{1,2},{2,3},{3,0},{4,5},{5,6},{6,7},{7,4},{8,9},{9,10},{10,1... | collective-permute-start | bytes 393224 | tf_op jit(solution)/shard_map/while/body/eval_jaxpr/ppermute | solution.py:13
  324.3 9.6 %collective-permute-start.1 = (f32[16,4096]{1,0:T(8,128)S(1)}, f32[16,4096]{1,0:T(8,128)S(1)}, u32[]{:S(2)}, u32[]{:S(2)}) collective-permute-start(f32[16,4096]{1,0:T(8,128)S(1)} %fusion.60), channel_id=1, source_target_pairs={{0,1},{1,2},{2,3},{3,0},{4,5},{5,6},{6,7},{7,4},{8,9},{9,10},{10,1... | collective-permute-start | bytes 786440 | tf_op jit(solution)/shard_map/while/body/eval_jaxpr/ppermute | solution.py:13
  324.3 9.6 %collective-permute-start = (bf16[16,4096]{1,0:T(8,128)(2,1)S(1)}, bf16[16,4096]{1,0:T(8,128)(2,1)S(1)}, u32[]{:S(2)}, u32[]{:S(2)}) collective-permute-start(bf16[16,4096]{1,0:T(8,128)(2,1)S(1)} %copy.27), channel_id=1, source_target_pairs={{0,1},{1,2},{2,3},{3,0},{4,5},{5,6},{6,7},{7,4},{8,9},{9,10},{10,1... | collective-permute-start | bytes 393224 | tf_op jit(solution)/shard_map/while/body/eval_jaxpr/ppermute | solution.py:13
  342.6 9.6 %collective-permute-start.1 = (f32[16,4096]{1,0:T(8,128)S(1)}, f32[16,4096]{1,0:T(8,128)S(1)}, u32[]{:S(2)}, u32[]{:S(2)}) collective-permute-start(f32[16,4096]{1,0:T(8,128)S(1)} %fusion.60), channel_id=1, source_target_pairs={{0,1},{1,2},{2,3},{3,0},{4,5},{5,6},{6,7},{7,4},{8,9},{9,10},{10,1... | collective-permute-start | bytes 786440 | tf_op jit(solution)/shard_map/while/body/eval_jaxpr/ppermute | solution.py:13
  342.6 9.6 %collective-permute-start = (bf16[16,4096]{1,0:T(8,128)(2,1)S(1)}, bf16[16,4096]{1,0:T(8,128)(2,1)S(1)}, u32[]{:S(2)}, u32[]{:S(2)}) collective-permute-start(bf16[16,4096]{1,0:T(8,128)(2,1)S(1)} %copy.27), channel_id=1, source_target_pairs={{0,1},{1,2},{2,3},{3,0},{4,5},{5,6},{6,7},{7,4},{8,9},{9,10},{10,1... | collective-permute-start | bytes 393224 | tf_op jit(solution)/shard_map/while/body/eval_jaxpr/ppermute | solution.py:13
